TPU v7x, 128 devices: a whole 4x4x4 slice. The times are simulated.
128 devices in a mesh: dp: 4 (over x), seq: 8 (over z, core), expert: 4 (over y).
Axes of the slice: x: 4, y: 4, z: 4, core: 2. Of those that a mesh axis runs over, the one named last changes fastest.
Arguments:
- x_in: bfloat16 [4096, 8192], P(('dp', 'seq'), 'expert'), parts along dimension 0, may hold values from -6 to 6
- z_in: bfloat16 [4096, 8192], P(('dp', 'seq'), 'expert'), parts along dimension 0, may hold values from -6 to 6
- step_raw: bfloat16 [4096, 8192], P(('dp', 'seq'), 'expert'), parts along dimension 0, may hold values from -4 to 4
- step_bias: float32 [8192], P('expert'), may hold values from -9 to -2
- decay_rate: float32 [16, 8192], P(None, 'expert'), may hold values from 0.5 to 4
- b_coef: bfloat16 [16, 4096], P(None, ('dp', 'seq')), parts along dimension 1, may hold values from -6 to 6
- c_coef: bfloat16 [16, 4096], P(None, ('dp', 'seq')), parts along dimension 1, may hold values from -6 to 6
- skip_gain: float32 [8192], P('expert'), may hold values from 0.5 to 1.5
- out_proj: bfloat16 [8192, 8192], P('expert', 'seq'), may hold values from -0.0625 to 0.0625
- residual: bfloat16 [4096, 8192], P(('dp', 'seq', 'expert')), parts along dimension 0, may hold values from -6 to 6
- norm_gain: float32 [8192], replicated, may hold values from 0.5 to 1.5
- router_weight: bfloat16 [8192, 16], replicated, may hold values from -0.0625 to 0.0625
- expert_ids: int32 [4096, 2], P(('dp', 'seq', 'expert')), parts along dimension 0, may hold values from 0 to 15, as said below
- gate_weight: bfloat16 [8192, 12288], P(None, ('seq', 'expert')), may hold values from -0.0625 to 0.0625
- up_weight: bfloat16 [8192, 12288], P(None, ('seq', 'expert')), may hold values from -0.0625 to 0.0625
- down_weight: bfloat16 [12288, 8192], P(('seq', 'expert')), may hold values from -0.0546875 to 0.0546875
Outputs:
- final: bfloat16 [4096, 8192], P(('dp', 'seq', 'expert')), parts along dimension 0
There are 4 independent parts, one for each index of `dp`. A program takes and returns all parts, laid end to end along the dimension named above; an argument that names none is the same for every part. Nothing has to cross between parts.
Inputs may be any that keep to these rules, and one draw needn't show every extreme that they name: `expert_ids`: each token names 2 different experts; among the 32 rows of one device at most 16 name expert 0 and at least one does; on some device exactly 16 do.
All inputs are finite; a program needn't handle non-finite values.
Results may differ from a plain program's by a relative error of at most 0.006.
Values may be sent and summed in bfloat16 or wider, within the bound.
No kernel may reach another device: no remote copies, remote signals or barrier semaphores. Data moves between devices by JAX's collectives and lax.ppermute only.
A program may use at most 192 MiB of HBM per device.

v0:
```python
import jax
import jax.numpy as jnp
from jax import lax
from jax.sharding import PartitionSpec as P

BLOCK = 128


def entering(value, axis, join, neutral):
    count, mine = (lax.axis_size(axis), lax.axis_index(axis))
    stacked = lax.all_gather(jnp.stack(value), axis)
    running = tuple((jnp.full_like(part, zero) for part, zero in zip(value, neutral)))
    for position in range(count - 1):
        longer = join(running, (stacked[position, 0], stacked[position, 1]))
        running = tuple((jnp.where(position < mine, new, old) for new, old in zip(longer, running)))
    return running


def pair_combine(early, later):
    return (early[0] * later[0], later[0] * early[1] + later[1])


def end_state(step_size, x_float, decay_rate, b_rows):

    def end_advance(state, inputs):
        step_now, x_now, b_now = inputs
        state = (
            jnp.exp(-step_now[None, :] * decay_rate) * state
            + (step_now * x_now)[None, :] * b_now[:, None]
        )
        return (state, None)

    start_state = jnp.zeros(decay_rate.shape, jnp.float32)
    final_state, _ = lax.scan(end_advance, start_state, (step_size, x_float, b_rows), unroll=8)
    return final_state


def scan_outputs(state_in, step_size, x_float, decay_rate, b_rows, c_rows, skip_gain):

    def scan_advance(state, inputs):
        step_now, x_now, b_now, c_now = inputs
        state = (
            jnp.exp(-step_now[None, :] * decay_rate) * state
            + (step_now * x_now)[None, :] * b_now[:, None]
        )
        y_now = jnp.sum(c_now[:, None] * state, axis=0) + skip_gain * x_now
        return (state, y_now)

    _, outputs = lax.scan(scan_advance, state_in, (step_size, x_float, b_rows, c_rows), unroll=8)
    return outputs


def on_device(
    x_in,
    z_in,
    step_raw,
    step_bias,
    decay_rate,
    b_coef,
    c_coef,
    skip_gain,
    out_proj,
    residual,
    norm_gain,
    router_weight,
    expert_ids,
    gate_weight,
    up_weight,
    down_weight,
):
    step_size = jax.nn.softplus(step_raw.astype(jnp.float32) + step_bias[None, :])
    x_float = x_in.astype(jnp.float32)
    b_rows = b_coef.astype(jnp.float32).T
    c_rows = c_coef.astype(jnp.float32).T
    state_end = end_state(step_size, x_float, decay_rate, b_rows)
    decay_end = jnp.exp(-decay_rate * jnp.sum(step_size, axis=0)[None, :])
    identity = (1.0, 0.0)
    carried = entering((decay_end, state_end), "seq", pair_combine, identity)
    state_in = carried[1]
    scanned = scan_outputs(state_in, step_size, x_float, decay_rate, b_rows, c_rows, skip_gain)
    gated = (scanned * jax.nn.silu(z_in.astype(jnp.float32))).astype(jnp.bfloat16)
    seq_count = lax.axis_size("seq")
    expert_count = lax.axis_size("expert")
    rows = residual.shape[0]
    gathered = lax.all_gather(gated, "seq", axis=0, tiled=True)
    gathered = gathered.reshape(seq_count, expert_count, rows, gated.shape[1])
    gathered = jnp.transpose(gathered, (1, 0, 2, 3)).reshape(-1, gated.shape[1])
    column_part = jnp.dot(gathered, out_proj, preferred_element_type=jnp.float32)
    summed = lax.psum_scatter(column_part, "expert", scatter_dimension=0, tiled=True)
    summed = summed.reshape(seq_count, rows, column_part.shape[1])
    swapped = lax.all_to_all(summed, "seq", split_axis=0, concat_axis=0, tiled=True)
    mamba_out = jnp.transpose(swapped, (1, 0, 2)).reshape(rows, -1)
    hidden = (residual.astype(jnp.float32) + mamba_out).astype(jnp.bfloat16)
    hidden_f = hidden.astype(jnp.float32)
    width_d = hidden.shape[1]
    scale_cols = width_d // BLOCK
    normed = (
        hidden_f
        * lax.rsqrt(jnp.mean(hidden_f * hidden_f, axis=-1, keepdims=True) + 1e-05)
        * norm_gain[None, :]
    )
    blocked = normed.reshape(rows, scale_cols, BLOCK)
    scales = (jnp.max(jnp.abs(blocked), axis=-1) / 448.0 + 1e-06).astype(jnp.bfloat16)
    quant = (blocked / scales.astype(jnp.float32)[..., None]).astype(jnp.bfloat16)
    restored = (
        (quant.astype(jnp.float32) * scales.astype(jnp.float32)[..., None])
        .astype(jnp.bfloat16)
        .reshape(rows, width_d)
    )
    experts = router_weight.shape[1]
    probs = jax.nn.sigmoid(jnp.dot(restored, router_weight, preferred_element_type=jnp.float32))
    picks = expert_ids[:, :, None] == jnp.arange(experts, dtype=jnp.int32)[None, None, :]
    chosen = jnp.sum(jnp.where(picks, probs[:, None, :], jnp.float32(0.0)), axis=-1)
    weights = chosen / jnp.sum(chosen, axis=-1, keepdims=True)
    coef = jnp.sum(jnp.where(expert_ids == 0, weights, jnp.float32(0.0)), axis=1)
    wanted = jnp.any(expert_ids == 0, axis=1)
    wanted_int = wanted.astype(jnp.int32)
    slot_pos = jnp.cumsum(wanted_int) - wanted_int
    capacity = rows // 2
    table = (
        (slot_pos[None, :] == jnp.arange(capacity, dtype=jnp.int32)[:, None]) & wanted[None, :]
    ).astype(jnp.bfloat16)
    send_rows = jnp.dot(table, restored, preferred_element_type=jnp.float32).astype(jnp.bfloat16)
    inputs = lax.all_gather(send_rows, ("seq", "expert"), axis=0, tiled=True)
    gate_value = jnp.dot(inputs, gate_weight, preferred_element_type=jnp.float32)
    up_value = jnp.dot(inputs, up_weight, preferred_element_type=jnp.float32)
    active = (jax.nn.silu(gate_value) * up_value).astype(jnp.bfloat16)
    own_sum = lax.psum_scatter(
        jnp.dot(active, down_weight, preferred_element_type=jnp.float32).astype(jnp.bfloat16),
        ("seq", "expert"),
        scatter_dimension=0,
        tiled=True,
    )
    returned = jnp.dot(table.T, own_sum, preferred_element_type=jnp.float32)
    return (hidden_f + coef[:, None] * returned).astype(jnp.bfloat16)


def solution(mesh):
    return jax.shard_map(
        on_device,
        mesh=mesh,
        in_specs=(
            P(("dp", "seq"), "expert"),
            P(("dp", "seq"), "expert"),
            P(("dp", "seq"), "expert"),
            P("expert"),
            P(None, "expert"),
            P(None, ("dp", "seq")),
            P(None, ("dp", "seq")),
            P("expert"),
            P("expert", "seq"),
            P(("dp", "seq", "expert"), None),
            P(),
            P(),
            P(("dp", "seq", "expert"), None),
            P(None, ("seq", "expert")),
            P(None, ("seq", "expert")),
            P(("seq", "expert"), None),
        ),
        out_specs=P(("dp", "seq", "expert"), None),
        check_vma=False,
    )
```

profile of v0, /device:TPU:0, one launch (start us, length us, event | category | flops | bytes accessed | tf_op | source)
XLA Modules:
  0.0 427.4 jit_solution(3741020597015307561)
XLA Ops:
  7.4 1.1 bitcast_convert_fusion
  8.5 1.7 fusion.66
  10.2 21.7 %while.24 = (s32[]{:T(128)}, f32[16,2048]{1,0:T(8,128)S(1)}, f32[16,8,2048]{2,1,0:T(8,128)S(1)}, f32[16,2048]{1,0:T(8,128)}, f32[16,8,2048]{2,1,0:T(8,128)S(1)},...) while((s32[]{:T(128)}, f32[16,2048]{1,0:T(8,128)S(1)}, ...), condition=%wide.region_2.3_spmd.clone, body=%wide.region_1.2_spmd.clone.sunk | while | flops 1114122 | bytes 789271 | solution.py:34
  10.4 1.2 fusion.117
  11.8 1.2 fusion.117
  13.2 1.2 fusion.117
  14.5 1.2 fusion.117
  15.9 1.2 fusion.117
  17.2 1.2 fusion.117
  18.6 1.2 fusion.117
  19.9 1.2 fusion.117
  21.3 1.2 fusion.117
  22.7 1.2 fusion.117
  24.0 1.2 fusion.117
  25.4 1.2 fusion.117
  26.7 1.2 fusion.117
  28.1 1.2 fusion.117
  29.5 1.2 fusion.117
  30.8 1.2 fusion.117
  33.9 28.0 %all-gather.9.cloned.1.call-done = f32[16,16,2048]{2,1,0:T(8,128)} async-done(((f32[2,16,2048]{2,1,0:T(8,128)}), f32[16,16,2048]{2,1,0:T(8,128)}) %all-gather.9.cloned.1.call-update) | async-done | bytes 2097168 | tf_op jit(solution)/shard_map/all_gather | solution.py:11
  61.8 1.6 fusion.69
  63.5 71.3 %while.23 = (s32[]{:T(128)}, f32[16,2048]{1,0:T(8,128)S(1)}, f32[16,8,2048]{2,1,0:T(8,128)}, f32[16,8,2048]{2,1,0:T(8,128)S(1)}, f32[16,2048]{1,0:T(8,128)}, /*i...) while((s32[]{:T(128)}, f32[16,2048]{1,0:T(8,128)S(1)}, ...), condition=%wide.region_12.13_spmd, body=%wide.region_3.12_spmd.sunk | while | flops 2408457 | bytes 2078409 | solution.py:49
  64.8 1.2 multiply_reduce_fusion.11
  66.0 1.1 multiply_reduce_fusion.12
  69.2 1.2 multiply_reduce_fusion.11
  70.5 1.1 multiply_reduce_fusion.12
  73.7 1.2 multiply_reduce_fusion.11
  74.9 1.1 multiply_reduce_fusion.12
  78.1 1.2 multiply_reduce_fusion.11
  79.4 1.1 multiply_reduce_fusion.12
  82.6 1.2 multiply_reduce_fusion.11
  83.8 1.1 multiply_reduce_fusion.12
  87.0 1.2 multiply_reduce_fusion.11
  88.3 1.1 multiply_reduce_fusion.12
  91.5 1.2 multiply_reduce_fusion.11
  92.7 1.1 multiply_reduce_fusion.12
  95.9 1.2 multiply_reduce_fusion.11
  97.2 1.1 multiply_reduce_fusion.12
  100.4 1.2 multiply_reduce_fusion.11
  101.6 1.1 multiply_reduce_fusion.12
  104.8 1.2 multiply_reduce_fusion.11
  106.1 1.1 multiply_reduce_fusion.12
  109.3 1.2 multiply_reduce_fusion.11
  110.5 1.1 multiply_reduce_fusion.12
  113.7 1.2 multiply_reduce_fusion.11
  115.0 1.1 multiply_reduce_fusion.12
  118.2 1.2 multiply_reduce_fusion.11
  119.4 1.1 multiply_reduce_fusion.12
  122.7 1.2 multiply_reduce_fusion.11
  123.9 1.1 multiply_reduce_fusion.12
  127.1 1.2 multiply_reduce_fusion.11
  131.6 1.2 multiply_reduce_fusion.11
  134.8 2.3 fusion.64
  137.2 32.6 %all-gather.5.cloned.1.call-done = bf16[1024,2048]{1,0:T(8,128)(2,1)} async-done(((bf16[128,2048]{1,0:T(8,128)(2,1)}), bf16[1024,2048]{1,0:T(8,128)(2,1)}) %all-gather.5.cloned.1.call-update) | async-done | bytes 4194320 | tf_op jit(solution)/shard_map/all_gather | solution.py:85
  169.8 2.7 copy.45
  173.2 6.0 %fusion.99 = f32[1024,1024]{1,0:T(8,128)} fusion(bf16[1024,2048]{1,0:T(8,128)(2,1)S(1)} %bitcast.416, bf16[2048,1024]{1,0:T(8,128)(2,1)S(1)} %copy-done.7), kind=kOutput, calls=%fused_computation.223 | convolution fusion | flops 4294967296 | bytes 12582912 | tf_op jit(solution)/shard_map/dot_general | solution.py:88
  179.3 46.8 %reduce-scatter.3.cloned.1.call-done = f32[256,1024]{1,0:T(8,128)} async-done(((f32[1024,1024]{1,0:T(8,128)}), f32[256,1024]{1,0:T(8,128)}) %reduce-scatter.3.cloned.1.call-update) | async-done | bytes 1048592 | tf_op jit(solution)/shard_map/reduce_scatter | solution.py:89
  226.1 4.4 %all-to-all-start = ((f32[8,32,1024]{2,1,0:T(8,128)}), f32[8,32,1024]{2,1,0:T(8,128)S(1)}, u32[]{:S(2)}, u32[]{:S(2)}) async-start(f32[8,32,1024]{2,1,0:T(8,128)} %bitcast.444), calls=%async_computation.1 | async-start | bytes 2097152 | tf_op jit(solution)/shard_map/all_to_all | solution.py:91
  230.9 15.6 %all-to-all-done = f32[8,32,1024]{2,1,0:T(8,128)S(1)} async-done(((f32[8,32,1024]{2,1,0:T(8,128)}), f32[8,32,1024]{2,1,0:T(8,128)S(1)}, u32[]{:S(2)}, u32[]{:S(2)}) %all-to-all-start) | async-done | bytes 1048608 | tf_op jit(solution)/shard_map/all_to_all | solution.py:91
  249.8 50.5 %all-gather.7.cloned.1.call-done = bf16[512,8192]{1,0:T(8,128)(2,1)} async-done(((bf16[16,8192]{1,0:T(8,128)(2,1)}), bf16[512,8192]{1,0:T(8,128)(2,1)}) %all-gather.7.cloned.1.call-update) | async-done | bytes 8388624 | tf_op jit(solution)/shard_map/all_gather | solution.py:124
  300.3 8.8 %fusion.100 = f32[512,384]{1,0:T(8,128)S(1)} fusion(bf16[512,8192]{1,0:T(8,128)(2,1)} %all-gather.7.cloned.1.call-done, bf16[8192,384]{1,0:T(8,128)(2,1)} %param.33), kind=kOutput, calls=%fused_computation.224 | convolution fusion | flops 3221225472 | bytes 15466496 | tf_op jit(solution)/shard_map/dot_general | solution.py:125
  309.1 17.1 %convolution_convert_fusion = bf16[512,8192]{1,0:T(8,128)(2,1)} fusion(bf16[384,8192]{1,0:T(8,128)(2,1)} %param.35, bf16[512,8192]{1,0:T(8,128)(2,1)} %all-gather.7.cloned.1.call-done, bf16[8192,384]{1,0:T(8,128)(2,1)} %param.34, f32[512,384]{1,0:T(8,128)S(1)} %fusion.100), kind=kOutput, calls=%fused_computation.132 | convolution fusion | flops 6447824896 | bytes 30146560 | tf_op jit(solution)/shard_map/dot_general | solution.py:129
  326.5 92.3 %reduce-scatter.5.cloned.1.call-done = bf16[16,8192]{1,0:T(8,128)(2,1)} async-done(((bf16[512,8192]{1,0:T(8,128)(2,1)}), bf16[16,8192]{1,0:T(8,128)(2,1)}) %reduce-scatter.5.cloned.1.call-update) | async-done | bytes 262160 | tf_op jit(solution)/shard_map/reduce_scatter | solution.py:128
  418.8 2.1 fusion.48
  (231 shorter events, 45.4 us)
Async XLA Ops:
  6.5 319.7 %copy-start = (bf16[8192,16]{0,1:T(8,128)(2,1)S(1)}, bf16[8192,16]{0,1:T(8,128)(2,1)}, u32[]{:S(2)}) copy-start(bf16[8192,16]{0,1:T(8,128)(2,1)} %param.31) | copy-start | bytes 786436
  6.5 27.2 %copy-start.5 = (bf16[16,128]{1,0:T(8,128)(2,1)S(1)}, bf16[16,128]{1,0:T(8,128)(2,1)}, u32[]{:S(2)}) copy-start(bf16[16,128]{1,0:T(8,128)(2,1)} %param.26) | copy-start | bytes 12292
  6.5 56.9 %copy-start.3 = (f32[2048]{0:T(1024)S(1)}, f32[2048]{0:T(1024)}, u32[]{:S(2)}) copy-start(f32[2048]{0:T(1024)} %param.27) | copy-start | bytes 24580
  6.5 55.3 %all-gather.9.cloned.1.call-start = ((), (), s32[]{:S(2)}) async-start(), calls=%async_computation.7 | async-start | bytes 2359296 | tf_op jit(solution)/shard_map/all_gather | solution.py:11
  33.7 136.1 %all-gather.5.cloned.1.call-start = ((), (), s32[]{:S(2)}) async-start(), calls=%async_computation.3 | async-start | bytes 4718592 | tf_op jit(solution)/shard_map/all_gather | solution.py:85
  63.5 71.3 %copy-start.2 = (bf16[128,2048]{1,0:T(8,128)(2,1)S(1)}, bf16[128,2048]{1,0:T(8,128)(2,1)}, u32[]{:S(2)}) copy-start(bf16[128,2048]{1,0:T(8,128)(2,1)} %param.21) | copy-start | bytes 1572868
  137.1 89.0 %reduce-scatter.3.cloned.1.call-start = ((), (), s32[]{:S(2)}) async-start(), calls=%async_computation.4 | async-start | bytes 5242880 | tf_op jit(solution)/shard_map/reduce_scatter | solution.py:89
  169.8 3.4 copy-start.7
  179.2 51.3 %copy-start.6 = (s32[32,2]{0,1:T(2,128)S(1)}, s32[32,2]{0,1:T(2,128)}, u32[]{:S(2)}) copy-start(s32[32,2]{0,1:T(2,128)} %param.32) | copy-start | bytes 772
  179.2 67.3 %copy-start.1 = (bf16[32,8192]{1,0:T(8,128)(2,1)S(1)}, bf16[32,8192]{1,0:T(8,128)(2,1)}, u32[]{:S(2)}) copy-start(bf16[32,8192]{1,0:T(8,128)(2,1)} %param.29) | copy-start | bytes 1572868
  179.2 67.6 %copy-start.4 = (f32[8192]{0:T(1024)S(1)}, f32[8192]{0:T(1024)}, u32[]{:S(2)}) copy-start(f32[8192]{0:T(1024)} %param.30) | copy-start | bytes 98308
  226.1 20.4 %all-to-all-start = ((f32[8,32,1024]{2,1,0:T(8,128)}), f32[8,32,1024]{2,1,0:T(8,128)S(1)}, u32[]{:S(2)}, u32[]{:S(2)}) async-start(f32[8,32,1024]{2,1,0:T(8,128)} %bitcast.444), calls=%async_computation.1 | async-start | bytes 2097152 | tf_op jit(solution)/shard_map/all_to_all | solution.py:91
  230.5 69.8 %all-gather.7.cloned.1.call-start = ((), (), s32[]{:S(2)}) async-start(), calls=%async_computation.5 | async-start | bytes 8650752 | tf_op jit(solution)/shard_map/all_gather | solution.py:124
  249.5 169.3 %reduce-scatter.5.cloned.1.call-start = ((), (), s32[]{:S(2)}) async-start(), calls=%async_computation.6 | async-start | bytes 8650752 | tf_op jit(solution)/shard_map/reduce_scatter | solution.py:128
Sparse Core Ops, SparseCore 0:
  33.8 27.9 all-gather.8
  137.2 32.4 all-gather.4
  179.4 46.6 reduce-scatter.2
  249.7 50.5 all-gather.6
  326.3 92.4 reduce-scatter.4
where the time goes:
time: 429 us; the launch traced here: 427 us
  waiting for transfers between devices  266 us (62%)
  other arithmetic  90.4 us (21%)
  matrix products  35.2 us (8%)
  local copies, waits for them, and re-layouts  16.7 us (4%)
  between operations  13.3 us (3%)
  starting transfers between devices  4.79 us (1%)
    reduce_scatter x1, waiting for transfers between devices, on_device(): lax.psum_scatter(jnp.dot(active, down_weight, preferred_element_type=jnp....  92.3 us
    reduce_sum x48, other arithmetic, scan_advance(): y_now = jnp.sum(c_now[:, None] * state, axis=0) + skip_gain * x_now  54.9 us
    all_gather x1, waiting for transfers between devices, on_device(): inputs = lax.all_gather(send_rows, ('seq', 'expert'), axis=0, tiled=True)  50.5 us
    reduce_scatter x1, waiting for transfers between devices, on_device(): lax.psum_scatter(column_part, 'expert', scatter_dimension=0, tiled=True)  46.8 us
    all_gather x1, waiting for transfers between devices, on_device(): gathered = lax.all_gather(gated, 'seq', axis=0, tiled=True)  32.6 us
    all_gather x1, waiting for transfers between devices, entering(): stacked = lax.all_gather(jnp.stack(value), axis)  28 us
    add x16, other arithmetic, end_advance(): jnp.exp(-step_now[None, :] * decay_rate) * state  18.6 us
    dot_general x1, matrix products, on_device(): jnp.dot(active, down_weight, preferred_element_type=jnp.float32)  17.1 us
  transfers between devices with their start and end apart: 6, of which 6 were waited for; matrix products, arithmetic and copies ran while one was open for 0% of the time, Pallas kernels for 0%

commit v1 on v0

--- a/solution.py
+++ b/solution.py
@@ -82,7 +82,9 @@
     seq_count = lax.axis_size("seq")
     expert_count = lax.axis_size("expert")
     rows = residual.shape[0]
-    gathered = lax.all_gather(gated, "seq", axis=0, tiled=True)
+    gathered = jnp.concatenate(
+        lax.all_to_all(jnp.stack([gated] * lax.axis_size("seq")), "seq", 0, 0), axis=0
+    )
     gathered = gathered.reshape(seq_count, expert_count, rows, gated.shape[1])
     gathered = jnp.transpose(gathered, (1, 0, 2, 3)).reshape(-1, gated.shape[1])
     column_part = jnp.dot(gathered, out_proj, preferred_element_type=jnp.float32)

time: 429 us -> 447 us (1.042)
  blocking collectives: 0 us -> 52.9 us
  waiting for transfers between devices: 266 us -> 233 us
    all_to_all x0 -> x1, blocking collectives: none -> 52.9 us  [on_device(): lax.all_to_all(jnp.stack([gated] * lax.axis_size('seq')), 'seq', 0, 0)]
    all_gather x1 -> x0, waiting for transfers between devices: 32.6 us -> none  [on_device(): gathered = lax.all_gather(gated, 'seq', axis=0, tiled=True)]
  transfers between devices with their start and end apart: 6 -> 5, of which waited for: 6 -> 5; matrix products, arithmetic and copies ran while one was open for 0% -> 0% of each run, Pallas kernels for 0% -> 0%
where the time goes in v1:
time: 447 us; the launch traced here: 446 us
  waiting for transfers between devices  233 us (52%)
  other arithmetic  89.7 us (20%)
  blocking collectives  52.9 us (12%)
  matrix products  35.2 us (8%)
  local copies, waits for them, and re-layouts  16 us (4%)
  between operations  13.3 us (3%)
  starting transfers between devices  4.72 us (1%)
    reduce_scatter x1, waiting for transfers between devices, on_device(): lax.psum_scatter(jnp.dot(active, down_weight, preferred_element_type=jnp....  92.3 us
    reduce_sum x48, other arithmetic, scan_advance(): y_now = jnp.sum(c_now[:, None] * state, axis=0) + skip_gain * x_now  54.9 us
    all_to_all x1, blocking collectives, on_device(): lax.all_to_all(jnp.stack([gated] * lax.axis_size('seq')), 'seq', 0, 0)  52.9 us
    all_gather x1, waiting for transfers between devices, on_device(): inputs = lax.all_gather(send_rows, ('seq', 'expert'), axis=0, tiled=True)  50.5 us
    reduce_scatter x1, waiting for transfers between devices, on_device(): lax.psum_scatter(column_part, 'expert', scatter_dimension=0, tiled=True)  46.3 us
    all_gather x1, waiting for transfers between devices, entering(): stacked = lax.all_gather(jnp.stack(value), axis)  28 us
    add x16, other arithmetic, end_advance(): jnp.exp(-step_now[None, :] * decay_rate) * state  18.7 us
    dot_general x1, matrix products, on_device(): jnp.dot(active, down_weight, preferred_element_type=jnp.float32)  17.1 us
  transfers between devices with their start and end apart: 5, of which 5 were waited for; matrix products, arithmetic and copies ran while one was open for 0% of the time, Pallas kernels for 0%

profile of v1, /device:TPU:0, one launch (start us, length us, event | category | flops | bytes accessed | tf_op | source)
XLA Modules:
  0.0 445.7 jit_solution(11347482442488431074)
XLA Ops:
  7.4 1.1 bitcast_convert_fusion
  8.5 1.7 fusion.66
  10.2 21.8 %while.24 = (s32[]{:T(128)}, f32[16,2048]{1,0:T(8,128)S(1)}, f32[16,8,2048]{2,1,0:T(8,128)S(1)}, f32[16,2048]{1,0:T(8,128)}, f32[16,8,2048]{2,1,0:T(8,128)S(1)},...) while((s32[]{:T(128)}, f32[16,2048]{1,0:T(8,128)S(1)}, ...), condition=%wide.region_2.3_spmd.clone, body=%wide.region_1.2_spmd.clone.sunk | while | flops 1114122 | bytes 789271 | solution.py:34
  10.4 1.2 fusion.117
  11.8 1.2 fusion.117
  13.2 1.2 fusion.117
  14.5 1.2 fusion.117
  15.9 1.2 fusion.117
  17.2 1.2 fusion.117
  18.6 1.2 fusion.117
  20.0 1.2 fusion.117
  21.3 1.2 fusion.117
  22.7 1.2 fusion.117
  24.1 1.2 fusion.117
  25.4 1.2 fusion.117
  26.8 1.2 fusion.117
  28.2 1.2 fusion.117
  29.5 1.2 fusion.117
  30.9 1.2 fusion.117
  34.0 28.0 %all-gather.6.cloned.1.call-done = f32[16,16,2048]{2,1,0:T(8,128)} async-done(((f32[2,16,2048]{2,1,0:T(8,128)}), f32[16,16,2048]{2,1,0:T(8,128)}) %all-gather.6.cloned.1.call-update) | async-done | bytes 2097168 | tf_op jit(solution)/shard_map/all_gather | solution.py:11
  61.9 1.6 fusion.69
  63.6 71.3 %while.23 = (s32[]{:T(128)}, f32[16,2048]{1,0:T(8,128)S(1)}, f32[16,8,2048]{2,1,0:T(8,128)}, f32[16,8,2048]{2,1,0:T(8,128)S(1)}, f32[16,2048]{1,0:T(8,128)}, /*i...) while((s32[]{:T(128)}, f32[16,2048]{1,0:T(8,128)S(1)}, ...), condition=%wide.region_12.13_spmd, body=%wide.region_3.12_spmd.sunk | while | flops 2408457 | bytes 2078409 | solution.py:49
  64.8 1.2 multiply_reduce_fusion.11
  66.1 1.1 multiply_reduce_fusion.12
  69.3 1.2 multiply_reduce_fusion.11
  70.5 1.1 multiply_reduce_fusion.12
  73.8 1.2 multiply_reduce_fusion.11
  75.0 1.1 multiply_reduce_fusion.12
  78.2 1.2 multiply_reduce_fusion.11
  79.4 1.1 multiply_reduce_fusion.12
  82.7 1.2 multiply_reduce_fusion.11
  83.9 1.1 multiply_reduce_fusion.12
  87.1 1.2 multiply_reduce_fusion.11
  88.3 1.1 multiply_reduce_fusion.12
  91.6 1.2 multiply_reduce_fusion.11
  92.8 1.1 multiply_reduce_fusion.12
  96.0 1.2 multiply_reduce_fusion.11
  97.2 1.1 multiply_reduce_fusion.12
  100.5 1.2 multiply_reduce_fusion.11
  101.7 1.1 multiply_reduce_fusion.12
  104.9 1.2 multiply_reduce_fusion.11
  106.2 1.1 multiply_reduce_fusion.12
  109.4 1.2 multiply_reduce_fusion.11
  110.6 1.1 multiply_reduce_fusion.12
  113.8 1.2 multiply_reduce_fusion.11
  115.1 1.1 multiply_reduce_fusion.12
  118.3 1.2 multiply_reduce_fusion.11
  119.5 1.1 multiply_reduce_fusion.12
  122.7 1.2 multiply_reduce_fusion.11
  124.0 1.1 multiply_reduce_fusion.12
  127.2 1.2 multiply_reduce_fusion.11
  131.7 1.2 multiply_reduce_fusion.11
  134.9 1.5 fusion.64
  136.9 52.9 %all_to_all.10 = bf16[8,128,2048]{2,1,0:T(8,128)(2,1)S(1)} all-to-all(bf16[8,128,2048]{2,1,0:T(8,128)(2,1)S(1)} %stack.11), channel_id=1, replica_groups=mesh['dp'=4,'seq'=8,'expert'=4] {'seq'}, dimensions={0} | all-to-all | bytes 8388608 | tf_op jit(solution)/shard_map/all_to_all | solution.py:86
  190.4 1.6 copy-done.7
  192.0 6.0 %fusion.99 = f32[1024,1024]{1,0:T(8,128)} fusion(bf16[1024,2048]{1,0:T(8,128)(2,1)S(1)} %bitcast.416, bf16[2048,1024]{1,0:T(8,128)(2,1)S(1)} %copy-done.7), kind=kOutput, calls=%fused_computation.223 | convolution fusion | flops 4294967296 | bytes 12582912 | tf_op jit(solution)/shard_map/dot_general | solution.py:90
  198.0 46.3 %reduce-scatter.3.cloned.1.call-done = f32[256,1024]{1,0:T(8,128)} async-done(((f32[1024,1024]{1,0:T(8,128)}), f32[256,1024]{1,0:T(8,128)}) %reduce-scatter.3.cloned.1.call-update) | async-done | bytes 1048592 | tf_op jit(solution)/shard_map/reduce_scatter | solution.py:91
  244.3 4.4 all-to-all-start.1
  249.1 15.6 %all-to-all-done.1 = f32[8,32,1024]{2,1,0:T(8,128)S(1)} async-done(((f32[8,32,1024]{2,1,0:T(8,128)}), f32[8,32,1024]{2,1,0:T(8,128)S(1)}, u32[]{:S(2)}, u32[]{:S(2)}) %all-to-all-start.1) | async-done | bytes 1048608 | tf_op jit(solution)/shard_map/all_to_all | solution.py:93
  268.0 50.5 %all-gather.4.cloned.1.call-done = bf16[512,8192]{1,0:T(8,128)(2,1)} async-done(((bf16[16,8192]{1,0:T(8,128)(2,1)}), bf16[512,8192]{1,0:T(8,128)(2,1)}) %all-gather.4.cloned.1.call-update) | async-done | bytes 8388624 | tf_op jit(solution)/shard_map/all_gather | solution.py:126
  318.5 8.8 %fusion.100 = f32[512,384]{1,0:T(8,128)S(1)} fusion(bf16[512,8192]{1,0:T(8,128)(2,1)} %all-gather.4.cloned.1.call-done, bf16[8192,384]{1,0:T(8,128)(2,1)} %param.33), kind=kOutput, calls=%fused_computation.224 | convolution fusion | flops 3221225472 | bytes 15466496 | tf_op jit(solution)/shard_map/dot_general | solution.py:127
  327.3 17.1 %convolution_convert_fusion = bf16[512,8192]{1,0:T(8,128)(2,1)} fusion(bf16[384,8192]{1,0:T(8,128)(2,1)} %param.35, bf16[512,8192]{1,0:T(8,128)(2,1)} %all-gather.4.cloned.1.call-done, bf16[8192,384]{1,0:T(8,128)(2,1)} %param.34, f32[512,384]{1,0:T(8,128)S(1)} %fusion.100), kind=kOutput, calls=%fused_computation.132 | convolution fusion | flops 6447824896 | bytes 30146560 | tf_op jit(solution)/shard_map/dot_general | solution.py:131
  344.8 92.3 %reduce-scatter.5.cloned.1.call-done = bf16[16,8192]{1,0:T(8,128)(2,1)} async-done(((bf16[512,8192]{1,0:T(8,128)(2,1)}), bf16[16,8192]{1,0:T(8,128)(2,1)}) %reduce-scatter.5.cloned.1.call-update) | async-done | bytes 262160 | tf_op jit(solution)/shard_map/reduce_scatter | solution.py:130
  437.1 2.1 fusion.48
  (230 shorter events, 45.6 us)
Async XLA Ops:
  6.5 337.9 %copy-start = (bf16[8192,16]{0,1:T(8,128)(2,1)S(1)}, bf16[8192,16]{0,1:T(8,128)(2,1)}, u32[]{:S(2)}) copy-start(bf16[8192,16]{0,1:T(8,128)(2,1)} %param.31) | copy-start | bytes 786436
  6.5 27.3 %copy-start.5 = (bf16[16,128]{1,0:T(8,128)(2,1)S(1)}, bf16[16,128]{1,0:T(8,128)(2,1)}, u32[]{:S(2)}) copy-start(bf16[16,128]{1,0:T(8,128)(2,1)} %param.26) | copy-start | bytes 12292
  6.5 57.0 %copy-start.3 = (f32[2048]{0:T(1024)S(1)}, f32[2048]{0:T(1024)}, u32[]{:S(2)}) copy-start(f32[2048]{0:T(1024)} %param.27) | copy-start | bytes 24580
  6.5 55.4 %all-gather.6.cloned.1.call-start = ((), (), s32[]{:S(2)}) async-start(), calls=%async_computation.7 | async-start | bytes 2359296 | tf_op jit(solution)/shard_map/all_gather | solution.py:11
  33.7 210.6 %reduce-scatter.3.cloned.1.call-start = ((), (), s32[]{:S(2)}) async-start(), calls=%async_computation.4 | async-start | bytes 5242880 | tf_op jit(solution)/shard_map/reduce_scatter | solution.py:91
  63.5 71.3 %copy-start.2 = (bf16[128,2048]{1,0:T(8,128)(2,1)S(1)}, bf16[128,2048]{1,0:T(8,128)(2,1)}, u32[]{:S(2)}) copy-start(bf16[128,2048]{1,0:T(8,128)(2,1)} %param.21) | copy-start | bytes 1572868
  189.8 2.2 copy-start.7
  198.0 50.8 %copy-start.6 = (s32[32,2]{0,1:T(2,128)S(1)}, s32[32,2]{0,1:T(2,128)}, u32[]{:S(2)}) copy-start(s32[32,2]{0,1:T(2,128)} %param.32) | copy-start | bytes 772
  198.0 66.8 %copy-start.1 = (bf16[32,8192]{1,0:T(8,128)(2,1)S(1)}, bf16[32,8192]{1,0:T(8,128)(2,1)}, u32[]{:S(2)}) copy-start(bf16[32,8192]{1,0:T(8,128)(2,1)} %param.29) | copy-start | bytes 1572868
  198.0 67.1 %copy-start.4 = (f32[8192]{0:T(1024)S(1)}, f32[8192]{0:T(1024)}, u32[]{:S(2)}) copy-start(f32[8192]{0:T(1024)} %param.30) | copy-start | bytes 98308
  244.3 20.3 %all-to-all-start.1 = ((f32[8,32,1024]{2,1,0:T(8,128)}), f32[8,32,1024]{2,1,0:T(8,128)S(1)}, u32[]{:S(2)}, u32[]{:S(2)}) async-start(f32[8,32,1024]{2,1,0:T(8,128)} %bitcast.444), calls=%async_computation.2 | async-start | bytes 2097152 | tf_op jit(solution)/shard_map/all_to_all | solution.py:93
  248.7 69.8 %all-gather.4.cloned.1.call-start = ((), (), s32[]{:S(2)}) async-start(), calls=%async_computation.5 | async-start | bytes 8650752 | tf_op jit(solution)/shard_map/all_gather | solution.py:126
  267.8 169.3 %reduce-scatter.5.cloned.1.call-start = ((), (), s32[]{:S(2)}) async-start(), calls=%async_computation.6 | async-start | bytes 8650752 | tf_op jit(solution)/shard_map/reduce_scatter | solution.py:130
Sparse Core Ops, SparseCore 0:
  33.9 27.9 all-gather.5
  198.1 46.1 reduce-scatter.2
  267.9 50.6 all-gather.3
  344.6 92.4 reduce-scatter.4
